TPU v7x, 256 devices: a whole 4x4x8 slice. The times are simulated.
256 devices in a mesh: dp: 16 (over z, x_lo), own: 16 (over x_hi, y, core).
Axes of the slice: x: 4 (x_hi: 2, x_lo: 2; x = x_hi * 2 + x_lo), y: 4, z: 8, core: 2. Of those that a mesh axis runs over, the one named last changes fastest.
Arguments:
- grads: float32 [16, 16, 1024, 1024], P('dp', None, 'own'), may hold values from -0.27 to 0.27
- owner_map: int32 [16], replicated, may hold values from 0 to 31, as said below
- stat_left: float32 [32, 1024, 1024], P('own', 'dp'), as said below
- stat_right: float32 [32, 1024, 1024], P('own', 'dp'), as said below
- root_left: bfloat16 [32, 1024, 1024], P('own', 'dp'), as said below
- root_right: bfloat16 [32, 1024, 1024], P('own', 'dp'), as said below
- master: float32 [32, 1024, 1024], P('own', 'dp'), may hold values from -4 to 4
- moment_first: float32 [32, 1024, 1024], P('own', 'dp'), may hold values from -0.6 to 0.6
- moment_second: float32 [32, 1024, 1024], P('own', 'dp'), may hold values from 0.001 to 1, as said below
Outputs:
- left_next: float32 [32, 1024, 1024], P('own', 'dp')
- right_next: float32 [32, 1024, 1024], P('own', 'dp')
- master_next: float32 [32, 1024, 1024], P('own', 'dp')
- first_next: float32 [32, 1024, 1024], P('own', 'dp')
- second_next: float32 [32, 1024, 1024], P('own', 'dp')
- weights_out: bfloat16 [16, 1024, 1024], P(None, ('dp', 'own'))
Inputs may be any that keep to these rules, and one draw needn't show every extreme that they name: `owner_map`: no two blocks share a slot. In every draw all 2 slots of some owner are taken, and so are slots 0 and 31. `root_left`: symmetric in its last two dimensions. `root_right`: symmetric in its last two dimensions. `stat_left`: symmetric in its last two dimensions. `stat_right`: symmetric in its last two dimensions. `moment_second`: Positive.
All inputs are finite; a program needn't handle non-finite values.
Results may differ from a plain program's by a relative error of at most 0.0045.
Values may be sent and summed in bfloat16 or wider, within the bound.
No kernel may reach another device: no remote copies, remote signals or barrier semaphores. Data moves between devices by JAX's collectives and lax.ppermute only.
A program may use at most 128 MiB of HBM per device.

v0:
```python
import jax
import jax.numpy as jnp
from jax import lax
from jax.sharding import PartitionSpec as P

stat_decay = 0.9
first_decay = 0.9
second_decay = 0.99
learn_rate = 0.25


def per_device(
    grads,
    owner_map,
    stat_left,
    stat_right,
    root_left,
    root_right,
    master,
    moment_first,
    moment_second,
):
    owners = lax.axis_size("own")
    slot_count = stat_left.shape[0]
    rows_dev = stat_left.shape[1]
    order_size = stat_left.shape[2]
    blocks = owner_map.shape[0]
    owned_slots = owners * slot_count
    highest = lax.Precision.HIGHEST
    matches = owner_map[:, None] == jnp.arange(owned_slots, dtype=jnp.int32)[None, :]
    occupied = jnp.any(matches, axis=0)
    block_of = jnp.sum(jnp.where(matches, jnp.arange(blocks, dtype=jnp.int32)[:, None], 0), axis=0)
    partials = grads[0]
    summed = lax.psum(partials, "dp")
    packed = jnp.where(occupied[:, None, None], jnp.take(summed, block_of, axis=0), 0.0)
    packed = packed.reshape(owners, slot_count, summed.shape[1], order_size)
    arrived = lax.all_to_all(
        packed.astype(jnp.bfloat16), "own", split_axis=0, concat_axis=2, tiled=True
    ).astype(packed.dtype)
    whole_grad = arrived.reshape(slot_count, order_size, order_size)
    first_row = lax.axis_index("dp") * rows_dev
    own_rows = lax.dynamic_slice_in_dim(whole_grad, first_row, rows_dev, 1)
    own_cols = lax.dynamic_slice_in_dim(whole_grad, first_row, rows_dev, 2)
    left_new = stat_decay * stat_left + (1.0 - stat_decay) * jnp.einsum(
        "srk,snk->srn", own_rows, whole_grad, precision=highest, preferred_element_type=jnp.float32
    )
    right_new = stat_decay * stat_right + (1.0 - stat_decay) * jnp.einsum(
        "skr,skn->srn", own_cols, whole_grad, precision=highest, preferred_element_type=jnp.float32
    )
    first_new = first_decay * moment_first + (1.0 - first_decay) * own_rows
    second_new = second_decay * moment_second + (1.0 - second_decay) * own_rows * own_rows
    adam_step = first_new / (jnp.sqrt(second_new) + 1e-08)
    rounded = whole_grad.astype(jnp.bfloat16)
    partial_product = jnp.einsum(
        "skn,srn->skr", rounded, root_right, preferred_element_type=jnp.float32
    ).astype(jnp.bfloat16)
    direction = jnp.einsum(
        "srk,skn->srn",
        root_left,
        lax.all_gather(partial_product, "dp", axis=2, tiled=True),
        preferred_element_type=jnp.float32,
    )
    square_sums = lax.psum(
        (jnp.sum(adam_step * adam_step, axis=(1, 2)), jnp.sum(direction * direction, axis=(1, 2))),
        "dp",
    )
    graft = jnp.sqrt(square_sums[0]) / (jnp.sqrt(square_sums[1]) + 1e-06)
    master_new = master - learn_rate * graft[:, None, None] * direction
    occupied_mine = lax.dynamic_slice_in_dim(
        occupied, lax.axis_index("own") * slot_count, slot_count
    )[:, None, None]
    left_next = jnp.where(occupied_mine, left_new, stat_left)
    right_next = jnp.where(occupied_mine, right_new, stat_right)
    master_next = jnp.where(occupied_mine, master_new, master)
    first_next = jnp.where(occupied_mine, first_new, moment_first)
    second_next = jnp.where(occupied_mine, second_new, moment_second)
    shares = master_new.astype(jnp.bfloat16).reshape(
        slot_count, owners, rows_dev // owners, order_size
    )
    delivered = lax.all_to_all(shares, "own", split_axis=1, concat_axis=0, tiled=True)
    delivered = delivered.reshape(owned_slots, rows_dev // owners, order_size)
    weights_out = jnp.take(delivered, owner_map, axis=0)
    return (left_next, right_next, master_next, first_next, second_next, weights_out)


def solution(mesh):
    return jax.shard_map(
        per_device,
        mesh=mesh,
        in_specs=(
            P("dp", None, "own", None),
            P(),
            P("own", "dp", None),
            P("own", "dp", None),
            P("own", "dp", None),
            P("own", "dp", None),
            P("own", "dp", None),
            P("own", "dp", None),
            P("own", "dp", None),
        ),
        out_specs=(
            P("own", "dp", None),
            P("own", "dp", None),
            P("own", "dp", None),
            P("own", "dp", None),
            P("own", "dp", None),
            P(None, ("dp", "own"), None),
        ),
        check_vma=False,
    )
```

profile of v0, /device:TPU:1, one launch (start us, length us, event | category | flops | bytes accessed | tf_op | source)
XLA Modules:
  0.0 420.0 jit_solution(211106581229123987)
XLA Ops:
  7.2 0.8 fusion.13
  8.0 0.7 select_reduce_fusion
  8.8 0.1 reduce_sum.32
  8.8 0.1 broadcast_in_dim.75
  9.0 179.9 %all-reduce.2 = bf16[16,64,1024]{2,1,0:T(8,128)(2,1)S(1)} all-reduce(f32[16,64,1024]{2,1,0:T(8,128)} %bitcast.52), channel_id=1, replica_groups=mesh['dp'=16,'own'=16] {'dp'}, use_global_device_ids=true, to_apply=%region_2.3 | all-reduce | flops 1048576 | bytes 6291456 | tf_op jit(solution)/shard_map/psum | solution.py:34
  188.9 2.8 gather_fusion
  191.6 4.3 %select_convert_fusion = bf16[16,2,64,1024]{3,2,1,0:T(8,128)(2,1)S(1)} fusion(bf16[16,2,64,1024]{3,2,1,0:T(8,128)(2,1)} %bitcast.51, pred[16,2]{1,0:T(8,128)(4,1)S(1)} %compare_and_fusion, pred[16,2]{1,0:T(8,128)(4,1)S(1)} %broadcast_in_dim.75), kind=kLoop, calls=%fused_computation.2 | loop fusion | flops 4194304 | bytes 8388672 | tf_op jit(solution)/shard_map/convert_element_type | solution.py:38
  195.9 61.4 %all_to_all.30 = bf16[16,2,64,1024]{3,2,1,0:T(8,128)(2,1)S(1)} all-to-all(bf16[16,2,64,1024]{3,2,1,0:T(8,128)(2,1)S(1)} %select_convert_fusion), channel_id=1, replica_groups=mesh['dp'=16,'own'=16] {'own'}, dimensions={0} | all-to-all | bytes 8388608 | tf_op jit(solution)/shard_map/all_to_all | solution.py:37
  257.4 0.7 copy.30
  258.1 1.9 copy-done.1
  260.1 2.1 convolution_convert_fusion
  262.3 2.4 fusion.7
  264.8 4.5 %fusion.3 = f32[2,64,1024]{2,1,0:T(8,128)} fusion(f32[2,64,1024]{2,1,0:T(8,128)S(1)} %copy-done.5, bf16[2,1024,1024]{2,1,0:T(8,128)(2,1)} %bitcast.49, s32[]{:T(128)S(6)} %select_n.69, pred[2]{0:T(512)(128)(4,1)S(1)} %dynamic_slice.13), kind=kOutput, calls=%fused_computation.8 | convolution fusion | flops 268959744 | bytes 5505030 | tf_op jit(solution)/shard_map/srk,snk->srn/dot_general | solution.py:44
  269.3 86.4 %all-gather.2.cloned.1.call-done = bf16[2,1024,1024]{1,2,0:T(8,128)(2,1)} async-done(((bf16[2,1024,64]{1,2,0:T(8,128)(2,1)}), bf16[2,1024,1024]{1,2,0:T(8,128)(2,1)}) %all-gather.2.cloned.1.call-update) | async-done | bytes 4194320 | tf_op jit(solution)/shard_map/all_gather | solution.py:60
  355.7 3.7 multiply_reduce_fusion
  359.4 26.4 %all-reduce = (f32[2]{0:T(128)S(1)}, f32[2]{0:T(128)S(1)}) all-reduce(f32[2]{0:T(128)S(1)} %get-tuple-element.13, f32[2]{0:T(128)S(1)} %get-tuple-element.9), channel_id=1, replica_groups=mesh['dp'=16,'own'=16] {'dp'}, use_global_device_ids=true, to_apply=%region_6.7 | all-reduce | flops 4 | bytes 32 | tf_op jit(solution)/shard_map/psum | solution.py:63
  385.8 1.0 fusion.10
  386.8 0.1 reshape.74
  386.9 0.8 copy.32
  387.7 15.3 %all-to-all-start.1 = ((bf16[2,16,4,1024]{3,2,0,1:T(4,128)(2,1)}), bf16[2,16,4,1024]{3,2,0,1:T(4,128)(2,1)S(1)}, u32[]{:S(2)}, u32[]{:S(2)}) async-start(bf16[2,16,4,1024]{3,2,0,1:T(4,128)(2,1)} %copy.32), calls=%async_computation.1 | async-start | bytes 524288 | tf_op jit(solution)/shard_map/all_to_all | solution.py:80
  403.0 4.3 %fusion.1 = f32[2,64,1024]{2,1,0:T(8,128)} fusion(f32[2,64,1024]{2,1,0:T(8,128)S(1)} %copy-done.2, bf16[2,1024,1024]{2,1,0:T(8,128)(2,1)} %bitcast.50, s32[]{:T(128)S(6)} %select_n.69, pred[2]{0:T(512)(128)(4,1)S(1)} %dynamic_slice.13), kind=kOutput, calls=%fused_computation.5 | convolution fusion | flops 268959744 | bytes 5767174 | tf_op jit(solution)/shard_map/skr,skn->srn/dot_general | solution.py:47
  407.3 4.4 %all-to-all-done.1 = bf16[2,16,4,1024]{3,2,0,1:T(4,128)(2,1)S(1)} async-done(((bf16[2,16,4,1024]{3,2,0,1:T(4,128)(2,1)}), bf16[2,16,4,1024]{3,2,0,1:T(4,128)(2,1)S(1)}, u32[]{:S(2)}, u32[]{:S(2)}) %all-to-all-start.1) | async-done | bytes 262176 | tf_op jit(solution)/shard_map/all_to_all | solution.py:80
  411.7 0.7 gather_fusion.1
  412.4 0.8 broadcast_select_fusion
  (27 shorter events, 0.2 us)
Async XLA Ops:
  7.2 348.5 %copy-start = (bf16[2,64,1024]{2,1,0:T(8,128)(2,1)S(1)}, bf16[2,64,1024]{2,1,0:T(8,128)(2,1)}, u32[]{:S(2)}) copy-start(bf16[2,64,1024]{2,1,0:T(8,128)(2,1)} %param.13) | copy-start | bytes 786436
  7.2 348.5 %all-gather.2.cloned.1.call-start = ((), (), s32[]{:S(2)}) async-start(), calls=%async_computation.2 | async-start | bytes 4456448 | tf_op jit(solution)/shard_map/all_gather | solution.py:60
  257.4 2.7 copy-start.7
  258.1 2.0 copy-start.1
  258.1 4.2 copy-start.8
  258.1 4.2 %copy-start.3 = (f32[2,64,1024]{2,1,0:T(8,128)S(1)}, f32[2,64,1024]{2,1,0:T(8,128)}, u32[]{:S(2)}) copy-start(f32[2,64,1024]{2,1,0:T(8,128)} %param.17) | copy-start | bytes 1572868
  258.1 4.2 %copy-start.4 = (f32[2,64,1024]{2,1,0:T(8,128)S(1)}, f32[2,64,1024]{2,1,0:T(8,128)}, u32[]{:S(2)}) copy-start(f32[2,64,1024]{2,1,0:T(8,128)} %param.16) | copy-start | bytes 1572868
  258.1 6.6 %copy-start.5 = (f32[2,64,1024]{2,1,0:T(8,128)S(1)}, f32[2,64,1024]{2,1,0:T(8,128)}, u32[]{:S(2)}) copy-start(f32[2,64,1024]{2,1,0:T(8,128)} %param.11) | copy-start | bytes 1572868
  264.8 121.1 %copy-start.6 = (f32[2,64,1024]{2,1,0:T(8,128)S(1)}, f32[2,64,1024]{2,1,0:T(8,128)}, u32[]{:S(2)}) copy-start(f32[2,64,1024]{2,1,0:T(8,128)} %param.15) | copy-start | bytes 1572868
  269.3 133.7 %copy-start.2 = (f32[2,64,1024]{2,1,0:T(8,128)S(1)}, f32[2,64,1024]{2,1,0:T(8,128)}, u32[]{:S(2)}) copy-start(f32[2,64,1024]{2,1,0:T(8,128)} %param.12) | copy-start | bytes 1572868
  387.7 24.0 %all-to-all-start.1 = ((bf16[2,16,4,1024]{3,2,0,1:T(4,128)(2,1)}), bf16[2,16,4,1024]{3,2,0,1:T(4,128)(2,1)S(1)}, u32[]{:S(2)}, u32[]{:S(2)}) async-start(bf16[2,16,4,1024]{3,2,0,1:T(4,128)(2,1)} %copy.32), calls=%async_computation.1 | async-start | bytes 524288 | tf_op jit(solution)/shard_map/all_to_all | solution.py:80
Sparse Core Ops, SparseCore 0:
  262.3 93.3 all-gather.1
where the time goes:
time: 420 us
  blocking collectives  268 us (64%)
  waiting for transfers between devices  90.8 us (22%)
  starting transfers between devices  15.3 us (4%)
  matrix products  14.6 us (3%)
  between operations  14.2 us (3%)
  other arithmetic  10.1 us (2%)
  local copies, waits for them, and re-layouts  7.27 us (2%)
    psum x1, blocking collectives, per_device(): summed = lax.psum(partials, 'dp')  180 us
    all_gather x1, waiting for transfers between devices, per_device(): lax.all_gather(partial_product, 'dp', axis=2, tiled=True)  86.4 us
    all_to_all x1, blocking collectives, per_device(): lax.all_to_all(packed.astype(jnp.bfloat16), 'own', split_axis=0, concat_a...  61.4 us
    psum x1, blocking collectives, per_device(): lax.psum((jnp.sum(adam_step * adam_step, axis=(1, 2)), jnp.sum(direction...  26.4 us
    all_to_all x1, starting transfers between devices, per_device(): lax.all_to_all(shares, 'own', split_axis=1, concat_axis=0, tiled=True)  15.3 us
  transfers between devices with their start and end apart: 2, of which 2 were waited for; matrix products, arithmetic and copies ran while one was open for 3% of the time, Pallas kernels for 0%

commit v1 on v0

--- a/solution.py
+++ b/solution.py
@@ -31,7 +31,8 @@
     occupied = jnp.any(matches, axis=0)
     block_of = jnp.sum(jnp.where(matches, jnp.arange(blocks, dtype=jnp.int32)[:, None], 0), axis=0)
     partials = grads[0]
-    summed = lax.psum(partials, "dp")
+    terms = lax.all_gather(partials, "dp")
+    summed = jnp.sum(terms, axis=0)
     packed = jnp.where(occupied[:, None, None], jnp.take(summed, block_of, axis=0), 0.0)
     packed = packed.reshape(owners, slot_count, summed.shape[1], order_size)
     arrived = lax.all_to_all(

time: 420 us -> 1630 us (3.88)
  waiting for transfers between devices: 90.8 us -> 1460 us
  blocking collectives: 268 us -> 84 us
  other arithmetic: 10.1 us -> 33.3 us
    all_gather x0 -> x1, waiting for transfers between devices: none -> 1370 us  [per_device(): terms = lax.all_gather(partials, 'dp')]
    psum x1 -> x0, blocking collectives: 180 us -> none  [per_device(): summed = lax.psum(partials, 'dp')]
    reduce_sum x0 -> x1, other arithmetic: none -> 21.2 us  [per_device(): summed = jnp.sum(terms, axis=0)]
  transfers between devices with their start and end apart: 2 -> 3, of which waited for: 2 -> 3; matrix products, arithmetic and copies ran while one was open for 3% -> 1% of each run, Pallas kernels for 0% -> 0%
where the time goes in v1:
time: 1630 us
  waiting for transfers between devices  1460 us (90%)
  blocking collectives  84 us (5%)
  other arithmetic  33.3 us (2%)
    all_gather x1, waiting for transfers between devices, per_device(): terms = lax.all_gather(partials, 'dp')  1370 us
    all_gather x1, waiting for transfers between devices, per_device(): lax.all_gather(partial_product, 'dp', axis=2, tiled=True)  84.7 us
    all_to_all x1, blocking collectives, per_device(): lax.all_to_all(packed.astype(jnp.bfloat16), 'own', split_axis=0, concat_a...  57.5 us
  transfers between devices with their start and end apart: 3, of which 3 were waited for; matrix products, arithmetic and copies ran while one was open for 1% of the time, Pallas kernels for 0%

profile of v1, /device:TPU:1, one launch (start us, length us, event | category | flops | bytes accessed | tf_op | source)
XLA Modules:
  0.0 1627.0 jit_solution(7457405055018599817)
XLA Ops:
  7.2 0.7 all-gather.3.cloned.1.call-update
  8.4 1367.2 %all-gather.3.cloned.1.call-done = f32[16,16,64,1024]{3,2,1,0:T(8,128)} async-done(((f32[1,16,64,1024]{3,2,1,0:T(8,128)}), f32[16,16,64,1024]{3,2,1,0:T(8,128)}) %all-gather.3.cloned.1.call-update) | async-done | bytes 67108880 | tf_op jit(solution)/shard_map/all_gather | solution.py:34
  1375.6 21.2 %reduce_sum.42 = bf16[16,64,1024]{2,1,0:T(8,128)(2,1)S(1)} reduce(f32[16,16,64,1024]{3,2,1,0:T(8,128)} %all-gather.3.cloned.1.call-done, f32[]{:T(128)} %constant.30.clone.1), dimensions={0}, to_apply=%region_2.3 | reduce | flops 15728640 | bytes 69206016 | tf_op jit(solution)/shard_map/reduce_sum | solution.py:35
  1396.8 2.8 gather_fusion
  1399.5 4.3 select_convert_fusion
  1403.8 57.5 %all_to_all.30 = bf16[16,2,64,1024]{3,2,1,0:T(8,128)(2,1)S(1)} all-to-all(bf16[16,2,64,1024]{3,2,1,0:T(8,128)(2,1)S(1)} %select_convert_fusion), channel_id=1, replica_groups=mesh['dp'=16,'own'=16] {'own'}, dimensions={0} | all-to-all | bytes 8388608 | tf_op jit(solution)/shard_map/all_to_all | solution.py:38
  1461.4 0.7 copy.29
  1462.1 1.5 copy-done.3
  1463.6 1.9 copy-done.1
  1465.5 2.1 convolution_convert_fusion
  1467.8 3.2 bitcast_convert_fusion
  1471.1 1.7 copy.31
  1472.7 2.6 fusion.10
  1475.3 2.2 fusion.3
  1477.5 84.7 %all-gather.5.cloned.1.call-done = bf16[2,1024,1024]{1,2,0:T(8,128)(2,1)} async-done(((bf16[2,1024,64]{1,2,0:T(8,128)(2,1)}), bf16[2,1024,1024]{1,2,0:T(8,128)(2,1)}) %all-gather.5.cloned.1.call-update) | async-done | bytes 4194320 | tf_op jit(solution)/shard_map/all_gather | solution.py:61
  1562.2 3.7 multiply_reduce_fusion
  1565.9 26.5 %all-reduce = (f32[2]{0:T(128)S(1)}, f32[2]{0:T(128)S(1)}) all-reduce(f32[2]{0:T(128)S(1)} %get-tuple-element.13, f32[2]{0:T(128)S(1)} %get-tuple-element.9), channel_id=1, replica_groups=mesh['dp'=16,'own'=16] {'dp'}, use_global_device_ids=true, to_apply=%region_6.7 | all-reduce | flops 4 | bytes 32 | tf_op jit(solution)/shard_map/psum | solution.py:64
  1592.4 1.0 fusion.7
  1593.5 0.8 copy.32
  1594.3 15.7 all-to-all-start.1
  1610.0 4.3 fusion.1
  1614.3 4.4 all-to-all-done.1
  1618.7 0.7 gather_fusion.1
  1619.4 0.8 broadcast_select_fusion
  (34 shorter events, 0.7 us)
Async XLA Ops:
  7.2 1555.1 %copy-start = (bf16[2,64,1024]{2,1,0:T(8,128)(2,1)S(1)}, bf16[2,64,1024]{2,1,0:T(8,128)(2,1)}, u32[]{:S(2)}) copy-start(bf16[2,64,1024]{2,1,0:T(8,128)(2,1)} %param.13) | copy-start | bytes 786436
  7.2 0.8 copy-start.9
  7.2 1368.4 %all-gather.3.cloned.1.call-start = ((), (), s32[]{:S(2)}) async-start(), calls=%async_computation.2 | async-start | bytes 71303168 | tf_op jit(solution)/shard_map/all_gather | solution.py:34
  7.9 1554.3 %all-gather.5.cloned.1.call-start = ((), (), s32[]{:S(2)}) async-start(), calls=%async_computation.3 | async-start | bytes 4456448 | tf_op jit(solution)/shard_map/all_gather | solution.py:61
  1461.4 2.2 copy-start.3
  1461.4 4.2 copy-start.8
  1463.6 1.9 copy-start.1
  1471.0 1.7 copy-start.7
  1471.0 4.3 copy-start.2
  1471.0 4.3 copy-start.5
  1475.3 117.1 %copy-start.6 = (f32[2,64,1024]{2,1,0:T(8,128)S(1)}, f32[2,64,1024]{2,1,0:T(8,128)}, u32[]{:S(2)}) copy-start(f32[2,64,1024]{2,1,0:T(8,128)} %param.15) | copy-start | bytes 1572868
  1477.5 132.5 %copy-start.4 = (f32[2,64,1024]{2,1,0:T(8,128)S(1)}, f32[2,64,1024]{2,1,0:T(8,128)}, u32[]{:S(2)}) copy-start(f32[2,64,1024]{2,1,0:T(8,128)} %param.12) | copy-start | bytes 1572868
  1594.3 24.4 %all-to-all-start.1 = ((bf16[2,16,4,1024]{3,2,0,1:T(4,128)(2,1)}), bf16[2,16,4,1024]{3,2,0,1:T(4,128)(2,1)S(1)}, u32[]{:S(2)}, u32[]{:S(2)}) async-start(bf16[2,16,4,1024]{3,2,0,1:T(4,128)(2,1)} %copy.32), calls=%async_computation.1 | async-start | bytes 524288 | tf_op jit(solution)/shard_map/all_to_all | solution.py:81
Sparse Core Ops, SparseCore 0:
  9.8 1365.7 all-gather.2
  1467.8 94.3 all-gather.4
